TPU v7x, 512 devices: a whole 4x4x16 slice. The times are simulated.
512 devices in a mesh: mx: 32 (over z, core), my: 4 (over y), layer: 4 (over x).
Axes of the slice: x: 4, y: 4, z: 16, core: 2. Of those that a mesh axis runs over, the one named last changes fastest.
Arguments:
- ssa_velocity: float32 [2, 2048, 1024], P(None, 'mx', 'my'), may hold values from -6 to 6
- shelf_viscosity: float32 [2048, 1024], P('mx', 'my'), may hold values from 0.3 to 3
- basal_friction: float32 [2048, 1024], P('mx', 'my'), may hold values from 0.1 to 3
- driving_stress: float32 [2, 2048, 1024], P(None, 'mx', 'my'), may hold values from -6 to 6
- stokes_velocity: float32 [3, 12, 512, 1024], P(None, 'layer', 'mx', 'my'), may hold values from -6 to 6
- ice_viscosity: float32 [12, 512, 1024], P('layer', 'mx', 'my'), may hold values from 0.3 to 3
- body_force: float32 [3, 12, 512, 1024], P(None, 'layer', 'mx', 'my'), may hold values from -6 to 6
- diagonals: int32 [512, 1024], P('mx', 'my'), may hold values 0 or 1
- element_matrix: float32 [18, 18], replicated, may hold values from -0.1 to 1.5, as said below
- iface_columns: int32 [128, 9, 128], P(('mx', 'my')), may hold values from -1 to 4095, as said below
- iface_nodes: int32 [128, 9, 128], P(('mx', 'my')), may hold values from -1 to 16383, as said below
Outputs:
- coupled_residual: float32 [2, 2048, 1024], P(None, 'mx', 'my')
- stokes_residual: float32 [3, 12, 512, 1024], P(None, 'layer', 'mx', 'my')
Inputs may be any that keep to these rules, and one draw needn't show every extreme that they name: `iface_columns`: slots toward blocks outside the map are empty; in each block and direction the live slots come first; all 128 slots toward a block's own direction (d = 4) are live; the live columns of one block are distinct. `iface_nodes`: slot (o, d, k) is live exactly where its partner slot (s, 8 - d, k) of iface_columns is live, s the block at offset d from o, and then names a node of o's 64 x 256 block (row-major). `element_matrix`: the diagonal dominates each row.
All inputs are finite; a program needn't handle non-finite values. No bound on the sum of `diagonals` on one device may be relied on, other than what follows from the above.
Results may differ from a plain program's by a relative error of at most 0.0001.
Values sent between devices are 32-bit elements; how exact they have to be, the bound alone decides.
No kernel may reach another device: no remote copies, remote signals or barrier semaphores. Data moves between devices by JAX's collectives and lax.ppermute only.
A program may use at most 64 MiB of HBM per device.

v0:
```python
import jax
import jax.numpy as jnp
from jax import lax
from jax.sharding import PartitionSpec as P


def with_halo(array, sides, width):
    for axis, dim in sides:
        devices, length = (lax.axis_size(axis), array.shape[dim])
        up = [(i, (i + 1) % devices) for i in range(devices - 1)]
        down = [(j, i) for i, j in up]
        last = lax.slice_in_dim(array, length - width, length, axis=dim)
        initial = lax.slice_in_dim(array, 0, width, axis=dim)
        before = lax.ppermute(last, axis, up)
        after = lax.ppermute(initial, axis, down)
        array = jnp.concatenate([before, array, after], axis=dim)
    return array


def cell_dx(plane):
    return 0.5 * (plane[1:, :-1] + plane[1:, 1:] - (plane[:-1, :-1] + plane[:-1, 1:]))


def cell_dy(plane):
    return 0.5 * (plane[:-1, 1:] + plane[1:, 1:] - (plane[:-1, :-1] + plane[1:, :-1]))


def shelf_residual(padded, friction, driving):
    u_field = padded[0]
    v_field = padded[1]
    h_field = padded[2]
    du_dx = cell_dx(u_field)
    du_dy = cell_dy(u_field)
    dv_dx = cell_dx(v_field)
    dv_dy = cell_dy(v_field)
    h_cell = 0.25 * (h_field[1:, :-1] + h_field[1:, 1:] + h_field[:-1, :-1] + h_field[:-1, 1:])
    tau_xx = h_cell * (4.0 * du_dx + 2.0 * dv_dy)
    tau_yy = h_cell * (4.0 * dv_dy + 2.0 * du_dx)
    tau_xy = h_cell * (du_dy + dv_dx)
    res_x = cell_dx(tau_xx) + cell_dy(tau_xy) - friction * u_field[1:-1, 1:-1] - driving[0]
    res_y = cell_dy(tau_yy) + cell_dx(tau_xy) - friction * v_field[1:-1, 1:-1] - driving[1]
    return jnp.stack([res_x, res_y])


def triangle(stiffness, lows, ups, weight):
    values = jnp.stack(
        [plane[comp] for group in (lows, ups) for comp in range(3) for plane in group]
    )
    viscous = (
        (lows[0][3] + lows[1][3] + lows[2][3] + ups[0][3] + ups[1][3] + ups[2][3]) / 6.0 * weight
    )
    response = (
        jnp.einsum("ab,bxy->axy", stiffness, values, precision=lax.Precision.HIGHEST) * viscous
    )
    return response.reshape((2, 3, 3) + response.shape[1:])


def cell_terms(lower, upper, flag_cells, stiffness, weight):
    low_a, low_b, low_c, low_d = (
        lower[:, :-1, :-1],
        lower[:, 1:, :-1],
        lower[:, :-1, 1:],
        lower[:, 1:, 1:],
    )
    up_a, up_b, up_c, up_d = (
        upper[:, :-1, :-1],
        upper[:, 1:, :-1],
        upper[:, :-1, 1:],
        upper[:, 1:, 1:],
    )
    main_diag = (flag_cells == 0)[None]
    low_far = jnp.where(main_diag, low_d, low_c)
    up_far = jnp.where(main_diag, up_d, up_c)
    low_near = jnp.where(main_diag, low_a, low_b)
    up_near = jnp.where(main_diag, up_a, up_b)
    tri_one = triangle(stiffness, (low_a, low_b, low_far), (up_a, up_b, up_far), weight)
    tri_two = triangle(stiffness, (low_near, low_d, low_c), (up_near, up_d, up_c), weight)
    result = []
    for height in range(2):
        resp_one = tri_one[height]
        resp_two = tri_two[height]
        corner_a = resp_one[:, 0] + jnp.where(main_diag, resp_two[:, 0], 0.0)
        corner_b = resp_one[:, 1] + jnp.where(main_diag, 0.0, resp_two[:, 0])
        corner_c = resp_two[:, 2] + jnp.where(main_diag, 0.0, resp_one[:, 2])
        corner_d = resp_two[:, 1] + jnp.where(main_diag, resp_one[:, 2], 0.0)
        result.append((corner_a, corner_b, corner_c, corner_d))
    return (result[0], result[1])


def add_corners(total, extra):
    if total is None:
        return extra
    return tuple((first_term + other_term for first_term, other_term in zip(total, extra)))


def scaled_by(corners, factor):
    return tuple((member * factor for member in corners))


def own_nodes(corners):
    corner_a, corner_b, corner_c, corner_d = corners
    return corner_a[:, 1:, 1:] + corner_b[:, :-1, 1:] + corner_c[:, 1:, :-1] + corner_d[:, :-1, :-1]


def per_device(
    ssa_velocity,
    shelf_viscosity,
    basal_friction,
    driving_stress,
    stokes_velocity,
    ice_viscosity,
    body_force,
    diagonals,
    element_matrix,
    iface_columns,
    iface_nodes,
):
    row_count = ssa_velocity.shape[1]
    col_count = ssa_velocity.shape[2]
    stacked = jnp.concatenate([ssa_velocity, shelf_viscosity[None]], 0)
    padded = with_halo(stacked, (("mx", 1), ("my", 2)), 1)
    shelf_res = shelf_residual(padded, basal_friction, driving_stress)
    owner_nodes = iface_nodes[0]
    node_live = owner_nodes >= 0
    flat_vel = ssa_velocity.reshape(2, row_count * col_count)
    outgoing = jnp.where(node_live[None], flat_vel[:, jnp.maximum(owner_nodes, 0)], 0.0)
    slot_count = outgoing.shape[2]
    grid_out = outgoing.reshape(2, 3, 3, slot_count)
    extended = with_halo(grid_out, (("mx", 1), ("my", 2)), 1)
    returned = extended[:, 0::2, 0::2].reshape(2, 9, slot_count)
    depth_count = stokes_velocity.shape[1]
    block_x = stokes_velocity.shape[2]
    block_y = stokes_velocity.shape[3]
    column_count = block_x * block_y
    columns = iface_columns[0]
    col_live = columns >= 0
    target = jnp.where(col_live, columns, column_count).reshape(-1)
    placed = (
        jnp.zeros((2, column_count + 1), jnp.float32)
        .at[:, target]
        .add(returned.reshape(2, -1))[:, :column_count]
    )
    marked = jnp.zeros((column_count + 1,), jnp.float32).at[target].add(1.0)[:column_count] > 0.0
    uv_part = jnp.where(
        marked.reshape(1, 1, block_x, block_y),
        placed.reshape(2, 1, block_x, block_y),
        stokes_velocity[:2],
    )
    stokes_field = jnp.concatenate([uv_part, stokes_velocity[2:3], ice_viscosity[None]], 0)
    planes = jnp.concatenate(
        [
            stokes_field.reshape(4 * depth_count, block_x, block_y),
            diagonals.astype(jnp.float32)[None],
        ],
        0,
    )
    widened = with_halo(planes, (("mx", 1), ("my", 2)), 1)
    flag_cells = widened[-1, :-1, :-1]
    field_ext = widened[:-1].reshape(4, depth_count, block_x + 2, block_y + 2)
    count_x = lax.axis_size("mx")
    count_y = lax.axis_size("my")
    place_x = lax.axis_index("mx")
    place_y = lax.axis_index("my")
    global_x = place_x * block_x + jnp.arange(block_x + 1, dtype=jnp.int32) - 1
    global_y = place_y * block_y + jnp.arange(block_y + 1, dtype=jnp.int32) - 1
    valid_x = (global_x >= 0) & (global_x <= count_x * block_x - 2)
    valid_y = (global_y >= 0) & (global_y <= count_y * block_y - 2)
    weight = (valid_x[:, None] & valid_y[None, :]).astype(jnp.float32)
    layer_index = lax.axis_index("layer")
    layer_count = lax.axis_size("layer")
    below_live = (layer_index > 0).astype(jnp.float32)
    above_live = (layer_index < layer_count - 1).astype(jnp.float32)
    extended_layers = with_halo(field_ext, (("layer", 1),), 1)
    collected = [None for height in range(depth_count)]
    for height in range(depth_count + 1):
        lower_part, upper_part = cell_terms(
            extended_layers[:, height],
            extended_layers[:, height + 1],
            flag_cells,
            element_matrix,
            weight,
        )
        if height > 0:
            if height == depth_count:
                lower_part = scaled_by(lower_part, above_live)
            collected[height - 1] = add_corners(collected[height - 1], lower_part)
        if height < depth_count:
            if height == 0:
                upper_part = scaled_by(upper_part, below_live)
            collected[height] = add_corners(collected[height], upper_part)
    owned = [own_nodes(corners) for corners in collected]
    stokes_residual = jnp.stack(owned, axis=1) - body_force
    depth_sum = jnp.sum(stokes_residual[:2], axis=1).reshape(2, column_count)
    bucket = jnp.where(col_live[None], depth_sum[:, jnp.maximum(columns, 0)], 0.0)
    depth_total = lax.psum(bucket, "layer")
    grid_back = depth_total.reshape(2, 3, 3, slot_count)
    extended_back = with_halo(grid_back, (("mx", 1), ("my", 2)), 1)
    at_owner = extended_back[:, 0::2, 0::2].reshape(2, 9, slot_count)
    node_index = jnp.where(node_live, owner_nodes, row_count * col_count).reshape(-1)
    node_force = (
        jnp.zeros((2, row_count * col_count + 1), jnp.float32)
        .at[:, node_index]
        .add(at_owner.reshape(2, -1))
    )
    node_force = node_force[:, : row_count * col_count].reshape(2, row_count, col_count)
    coupled_residual = shelf_res - node_force
    return (coupled_residual, stokes_residual)


def solution(mesh):
    return jax.shard_map(
        per_device,
        mesh=mesh,
        in_specs=(
            P(None, "mx", "my"),
            P("mx", "my"),
            P("mx", "my"),
            P(None, "mx", "my"),
            P(None, "layer", "mx", "my"),
            P("layer", "mx", "my"),
            P(None, "layer", "mx", "my"),
            P("mx", "my"),
            P(),
            P(("mx", "my"), None, None),
            P(("mx", "my"), None, None),
        ),
        out_specs=(P(None, "mx", "my"), P(None, "layer", "mx", "my")),
        check_vma=False,
    )
```

profile of v0, /device:TPU:97, one launch (start us, length us, event | category | flops | bytes accessed | tf_op | source)
XLA Modules:
  0.0 201.1 jit_solution(2747815549716672843)
XLA Ops:
  2.9 5.5 %copy.172 = f32[2,64,256]{0,2,1:T(8,128)} copy(f32[2,64,256]{2,1,0:T(8,128)} %param.11) | data formatting | bytes 262144 | tf_op args[0]
  9.0 5.8 %gather_fusion = f32[1152,2]{1,0:T(8,128)S(1)} fusion(f32[2,16384]{0,1:T(8,128)} %bitcast.297, s32[2048]{0:T(1024)S(1)} %get-tuple-element.199), kind=kCustom, calls=%fused_computation | custom fusion | bytes 23040 | tf_op jit(solution)/shard_map/gather | solution.py:126
  15.1 5.3 %collective-permute-start.4 = (f32[2,1,3,128]{3,0,2,1:T(2,128)S(1)}, f32[2,1,3,128]{3,0,2,1:T(2,128)S(1)}, u32[]{:S(2)}, u32[]{:S(2)}) collective-permute-start(f32[2,1,3,128]{3,0,2,1:T(2,128)S(1)} %get-tuple-element.196), channel_id=1, source_target_pairs={{0,16},{16,32},{32,48},{48,64},{64,80},{80,96},{96,112},{112,128},... | collective-permute-start | bytes 9224 | tf_op jit(solution)/shard_map/ppermute | solution.py:14
  20.5 1.9 collective-permute-start.5
  22.4 4.9 %collective-permute-start = (f32[3,1,256]{2,1,0:T(1,128)S(1)}, f32[3,1,256]{2,1,0:T(1,128)S(1)}, u32[]{:S(2)}, u32[]{:S(2)}) collective-permute-start(f32[3,1,256]{2,1,0:T(1,128)S(1)} %get-tuple-element.76), channel_id=1, source_target_pairs={{0,16},{16,32},{32,48},{48,64},{64,80},{80,96},{96,112},{112,128},... | collective-permute-start | bytes 9224 | tf_op jit(solution)/shard_map/ppermute | solution.py:14
  27.3 1.9 collective-permute-start.1
  29.9 8.7 %scatter_custom_fusion = f32[4097]{0:T(1024)S(1)} fusion(s32[1152]{0:T(1024)S(1)} %fusion.75, f32[1152]{0:T(1024)S(1)} %broadcast.299, f32[]{:T(128)} %constant.32.clone.1), kind=kCustom, calls=%fused_computation.252 | custom fusion | flops 1152 | bytes 16392 | tf_op jit(solution)/shard_map/scatter-add | solution.py:143
  39.4 2.8 %collective-permute-start.2 = (f32[3,66,1]{2,1,0:T(8,128)S(1)}, f32[3,66,1]{2,1,0:T(8,128)S(1)}, u32[]{:S(2)}, u32[]{:S(2)}) collective-permute-start(f32[3,66,1]{2,1,0:T(8,128)S(1)} %get-tuple-element.74), channel_id=1, source_target_pairs={{0,4},{4,8},{8,12},{1,5},{5,9},{9,13},{2,6},{6,10},{10,14},{3,7},{... | collective-permute-start | bytes 2384 | tf_op jit(solution)/shard_map/ppermute | solution.py:14
  43.5 4.0 %collective-permute-start.6 = (f32[2,5,1,128]{3,0,2,1:T(2,128)S(1)}, f32[2,5,1,128]{3,0,2,1:T(2,128)S(1)}, u32[]{:S(2)}, u32[]{:S(2)}) collective-permute-start(f32[2,5,1,128]{3,0,2,1:T(2,128)S(1)} %get-tuple-element.182), channel_id=1, source_target_pairs={{0,4},{4,8},{8,12},{1,5},{5,9},{9,13},{2,6},{6,10},{10,14},{3,7},{... | collective-permute-start | bytes 15368 | tf_op jit(solution)/shard_map/ppermute | solution.py:14
  49.1 2.8 %collective-permute-done.7 = f32[2,5,1,128]{3,0,2,1:T(2,128)S(1)} collective-permute-done((f32[2,5,1,128]{3,0,2,1:T(2,128)S(1)}, f32[2,5,1,128]{3,0,2,1:T(2,128)S(1)}, u32[]{:S(2)}, u32[]{:S(2)}) %collective-permute-start.7) | collective-permute-done | bytes 5152 | tf_op jit(solution)/shard_map/ppermute | solution.py:15
  52.2 10.6 %scatter_custom_fusion.1 = f32[2,4097]{0,1:T(8,128)S(1)} fusion(s32[1152]{0:T(1024)S(1)} %fusion.75, f32[1152,2]{1,0:T(8,128)S(1)} %copy.174, f32[]{:T(128)} %constant.32.clone.1), kind=kCustom, calls=%fused_computation.23 | custom fusion | flops 2304 | bytes 32780 | tf_op jit(solution)/shard_map/scatter-add | solution.py:141
  64.3 2.2 %copy.175 = f32[2,16,256]{2,1,0:T(8,128)S(1)} copy(f32[2,16,256]{0,2,1:T(8,128)} %bitcast.298) | data formatting | bytes 65536 | tf_op jit(solution)/shard_map/jit(_where)/broadcast_in_dim | solution.py:144
  66.7 7.0 %collective-permute-start.8 = (f32[13,1,256]{2,0,1:T(8,128)S(1)}, f32[13,1,256]{2,0,1:T(8,128)S(1)}, u32[]{:S(2)}, u32[]{:S(2)}) collective-permute-start(f32[13,1,256]{2,0,1:T(8,128)S(1)} %get-tuple-element.64), channel_id=1, source_target_pairs={{0,16},{16,32},{32,48},{48,64},{64,80},{80,96},{96,112},{112,128},... | collective-permute-start | bytes 39944 | tf_op jit(solution)/shard_map/ppermute | solution.py:14
  73.6 1.9 collective-permute-start.9
  75.8 4.1 %collective-permute-done.9 = f32[13,1,256]{2,0,1:T(8,128)S(1)} collective-permute-done((f32[13,1,256]{2,0,1:T(8,128)S(1)}, f32[13,1,256]{2,0,1:T(8,128)S(1)}, u32[]{:S(2)}, u32[]{:S(2)}) %collective-permute-start.9) | collective-permute-done | bytes 13344 | tf_op jit(solution)/shard_map/ppermute | solution.py:15
  80.1 2.7 %collective-permute-start.10 = (f32[13,18,1]{2,0,1:T(8,128)S(1)}, f32[13,18,1]{2,0,1:T(8,128)S(1)}, u32[]{:S(2)}, u32[]{:S(2)}) collective-permute-start(f32[13,18,1]{2,0,1:T(8,128)S(1)} %get-tuple-element.62), channel_id=1, source_target_pairs={{0,4},{4,8},{8,12},{1,5},{5,9},{9,13},{2,6},{6,10},{10,14},{3,7},{... | collective-permute-start | bytes 2816 | tf_op jit(solution)/shard_map/ppermute | solution.py:14
  84.9 3.8 %collective-permute-done.11 = f32[13,18,1]{2,0,1:T(8,128)S(1)} collective-permute-done((f32[13,18,1]{2,0,1:T(8,128)S(1)}, f32[13,18,1]{2,0,1:T(8,128)S(1)}, u32[]{:S(2)}, u32[]{:S(2)}) %collective-permute-start.11) | collective-permute-done | bytes 968 | tf_op jit(solution)/shard_map/ppermute | solution.py:15
  89.2 3.1 %collective-permute-start.12 = (f32[4,1,18,258]{3,0,2,1:T(4,128)S(1)}, f32[4,1,18,258]{3,0,2,1:T(4,128)S(1)}, u32[]{:S(2)}, u32[]{:S(2)}) collective-permute-start(f32[4,1,18,258]{3,0,2,1:T(4,128)S(1)} %copy.245), channel_id=1, source_target_pairs={{0,1},{1,2},{2,3},{4,5},{5,6},{6,7},{8,9},{9,10},{10,11},{12,13},{... | collective-permute-start | bytes 222920 | tf_op jit(solution)/shard_map/ppermute | solution.py:14
  103.4 1.8 and_select_fusion.1
  105.9 2.2 %stack.48 = f32[18,17,257]{2,0,1:T(8,128)S(1)} concatenate(f32[1,17,257]{2,0,1:T(1,128)} %get-tuple-element.106, f32[1,17,257]{2,0,1:T(1,128)} %get-tuple-element.105, f32[1,17,257]{2,0,1:T(1,128)} %get-tuple-element.152, f32[1,17,257]{2,0,1:T(1,128)} %get-tuple-element.103, f32[1,17,257]{2,0,1:T(1,128)S(1)} %get-tuple-element.102, f32[1,17,257]{2,0,1:T(1,128)} %get-tuple-element.151, ...), dimensions={0} | concatenate | bytes 629136 | tf_op jit(solution)/shard_map/stack | solution.py:46
  123.0 1.5 stack.54
  126.8 2.3 %stack.56 = f32[18,17,257]{2,0,1:T(8,128)S(1)} concatenate(f32[1,17,257]{2,0,1:T(1,128)S(1)} %get-tuple-element.142, f32[1,17,257]{2,0,1:T(1,128)S(1)} %get-tuple-element.141, f32[1,17,257]{2,0,1:T(1,128)S(1)} %copy-done.5, f32[1,17,257]{2,0,1:T(1,128)S(1)} %get-tuple-element.140, f32[1,17,257]{2,0,1:T(1,128)S(1)} %get-tuple-element.139, f32[1,17,257]{2,0,1:T(1,128)S(1)} %get-tuple-element.166, ...), dimensions={0} | concatenate | bytes 629136 | tf_op jit(solution)/shard_map/stack | solution.py:46
  132.1 2.3 %stack.57 = f32[18,17,257]{2,0,1:T(8,128)S(1)} concatenate(f32[1,17,257]{2,0,1:T(1,128)S(1)} %get-tuple-element.176, f32[1,17,257]{2,0,1:T(1,128)S(1)} %get-tuple-element.137, f32[1,17,257]{2,0,1:T(1,128)S(1)} %get-tuple-element.118, f32[1,17,257]{2,0,1:T(1,128)S(1)} %get-tuple-element.175, f32[1,17,257]{2,0,1:T(1,128)S(1)} %get-tuple-element.117, ...), dimensions={0} | concatenate | bytes 629136 | tf_op jit(solution)/shard_map/stack | solution.py:46
  140.8 2.9 %gather_fusion.1 = f32[1152,2]{1,0:T(8,128)S(1)} fusion(f32[2,4096]{0,1:T(8,128)S(1)} %bitcast.305, s32[2048]{0:T(1024)} %get-tuple-element.198), kind=kCustom, calls=%fused_computation.1 | custom fusion | bytes 23040 | tf_op jit(solution)/shard_map/gather | solution.py:194
  144.8 9.6 %psum.7 = f32[2,3,3,128]{3,0,2,1:T(2,128)S(1)} all-reduce(f32[2,3,3,128]{3,0,2,1:T(2,128)S(1)} %bitcast.339), channel_id=1, replica_groups=mesh['mx'=32,'my'=4,'layer'=4] {'layer'}, use_global_device_ids=true, to_apply=%region_3.4 | all-reduce | flops 2304 | bytes 18432 | tf_op jit(solution)/shard_map/psum | solution.py:195
  154.4 5.9 %collective-permute-start.14 = (f32[2,1,3,128]{3,0,2,1:T(2,128)S(1)}, f32[2,1,3,128]{3,0,2,1:T(2,128)S(1)}, u32[]{:S(2)}, u32[]{:S(2)}) collective-permute-start(f32[2,1,3,128]{3,0,2,1:T(2,128)S(1)} %get-tuple-element.185), channel_id=1, source_target_pairs={{0,16},{16,32},{32,48},{48,64},{64,80},{80,96},{96,112},{112,128},... | collective-permute-start | bytes 9224 | tf_op jit(solution)/shard_map/ppermute | solution.py:14
  161.4 1.9 collective-permute-start.15
  163.3 4.2 %collective-permute-done.15 = f32[2,1,3,128]{3,0,2,1:T(2,128)S(1)} collective-permute-done((f32[2,1,3,128]{3,0,2,1:T(2,128)S(1)}, f32[2,1,3,128]{3,0,2,1:T(2,128)S(1)}, u32[]{:S(2)}, u32[]{:S(2)}) %collective-permute-start.15) | collective-permute-done | bytes 3104 | tf_op jit(solution)/shard_map/ppermute | solution.py:15
  167.5 3.3 %collective-permute-start.16 = (f32[2,5,1,128]{3,0,2,1:T(2,128)S(1)}, f32[2,5,1,128]{3,0,2,1:T(2,128)S(1)}, u32[]{:S(2)}, u32[]{:S(2)}) collective-permute-start(f32[2,5,1,128]{3,0,2,1:T(2,128)S(1)} %get-tuple-element.180), channel_id=1, source_target_pairs={{0,4},{4,8},{8,12},{1,5},{5,9},{9,13},{2,6},{6,10},{10,14},{3,7},{... | collective-permute-start | bytes 15368 | tf_op jit(solution)/shard_map/ppermute | solution.py:14
  175.5 14.0 %scatter_custom_fusion.2 = f32[2,16385]{0,1:T(8,128)} fusion(s32[1152]{0:T(1024)} %fusion.74, f32[1152,2]{1,0:T(8,128)S(1)} %copy.231, f32[]{:T(128)} %constant.32.clone.1), kind=kCustom, calls=%fused_computation.5 | custom fusion | flops 2304 | bytes 131592 | tf_op jit(solution)/shard_map/scatter-add | solution.py:203
  189.5 5.7 %slice.1543 = f32[2,16384]{0,1:T(8,128)} slice(f32[2,16385]{0,1:T(8,128)} %scatter_custom_fusion.2), slice={[0:2], [0:16384]} | slice | bytes 262144 | tf_op jit(solution)/shard_map/slice | solution.py:205
  195.2 5.2 %copy.232 = f32[2,64,256]{2,1,0:T(8,128)S(1)} copy(f32[2,64,256]{0,2,1:T(8,128)} %bitcast.284) | data formatting | bytes 262144 | tf_op jit(solution)/shard_map/reshape | solution.py:205
  (213 shorter events, 57.3 us)
Async XLA Ops:
  0.6 107.5 %copy-start = (f32[18,18]{1,0:T(8,128)S(1)}, f32[18,18]{1,0:T(8,128)}, u32[]{:S(2)}) copy-start(f32[18,18]{1,0:T(8,128)} %param.19) | copy-start | bytes 3892
  0.6 28.6 %copy-start.23 = (s32[1,9,128]{2,0,1:T(1,128)S(1)}, s32[1,9,128]{2,0,1:T(1,128)}, u32[]{:S(2)}) copy-start(s32[1,9,128]{2,0,1:T(1,128)} %param.21) | copy-start | bytes 13828
  0.7 28.6 %copy-start.22 = (s32[1,9,128]{2,0,1:T(1,128)S(1)}, s32[1,9,128]{2,0,1:T(1,128)}, u32[]{:S(2)}) copy-start(s32[1,9,128]{2,0,1:T(1,128)} %param.20) | copy-start | bytes 13828
  0.7 21.7 %copy-start.1 = (f32[2,64,256]{2,1,0:T(8,128)S(1)}, f32[2,64,256]{2,1,0:T(8,128)}, u32[]{:S(2)}) copy-start(f32[2,64,256]{2,1,0:T(8,128)} %param.11) | copy-start | bytes 393220
  0.7 21.7 %copy-start.2 = (f32[64,256]{1,0:T(8,128)S(1)}, f32[64,256]{1,0:T(8,128)}, u32[]{:S(2)}) copy-start(f32[64,256]{1,0:T(8,128)} %param.12) | copy-start | bytes 196612
  0.7 38.0 %copy-start.24 = (s32[16,256]{1,0:T(8,128)S(1)}, s32[16,256]{1,0:T(8,128)}, u32[]{:S(2)}) copy-start(s32[16,256]{1,0:T(8,128)} %param.18) | copy-start | bytes 49156
  8.4 58.0 %copy-start.10 = (f32[3,3,16,256]{3,2,1,0:T(8,128)S(1)}, f32[3,3,16,256]{3,2,1,0:T(8,128)}, u32[]{:S(2)}) copy-start(f32[3,3,16,256]{3,2,1,0:T(8,128)} %param.15) | copy-start | bytes 442372
  8.4 58.1 %slice-start = ((f32[3,3,16,256]{3,2,1,0:T(8,128)}), f32[1,3,16,256]{3,2,1,0:T(8,128)S(1)}, s32[]{:S(2)}) async-start(f32[3,3,16,256]{3,2,1,0:T(8,128)} %param.15), calls=%async_computation | async-start | bytes 98304 | tf_op jit(solution)/shard_map/slice | solution.py:149
  8.4 58.1 %copy-start.21 = (f32[3,16,256]{2,1,0:T(8,128)S(1)}, f32[3,16,256]{2,1,0:T(8,128)}, u32[]{:S(2)}) copy-start(f32[3,16,256]{2,1,0:T(8,128)} %param.16) | copy-start | bytes 147460
  15.1 28.4 %collective-permute-start.4 = (f32[2,1,3,128]{3,0,2,1:T(2,128)S(1)}, f32[2,1,3,128]{3,0,2,1:T(2,128)S(1)}, u32[]{:S(2)}, u32[]{:S(2)}) collective-permute-start(f32[2,1,3,128]{3,0,2,1:T(2,128)S(1)} %get-tuple-element.196), channel_id=1, source_target_pairs={{0,16},{16,32},{32,48},{48,64},{64,80},{80,96},{96,112},{112,128},... | collective-permute-start | bytes 9224 | tf_op jit(solution)/shard_map/ppermute | solution.py:14
  20.5 23.1 %collective-permute-start.5 = (f32[2,1,3,128]{3,0,2,1:T(2,128)S(1)}, f32[2,1,3,128]{3,0,2,1:T(2,128)S(1)}, u32[]{:S(2)}, u32[]{:S(2)}) collective-permute-start(f32[2,1,3,128]{3,0,2,1:T(2,128)S(1)} %get-tuple-element.197), channel_id=1, source_target_pairs={{16,0},{32,16},{48,32},{64,48},{80,64},{96,80},{112,96},{128,112},... | collective-permute-start | bytes 9224 | tf_op jit(solution)/shard_map/ppermute | solution.py:15
  22.4 16.9 %collective-permute-start = (f32[3,1,256]{2,1,0:T(1,128)S(1)}, f32[3,1,256]{2,1,0:T(1,128)S(1)}, u32[]{:S(2)}, u32[]{:S(2)}) collective-permute-start(f32[3,1,256]{2,1,0:T(1,128)S(1)} %get-tuple-element.76), channel_id=1, source_target_pairs={{0,16},{16,32},{32,48},{48,64},{64,80},{80,96},{96,112},{112,128},... | collective-permute-start | bytes 9224 | tf_op jit(solution)/shard_map/ppermute | solution.py:14
  27.3 12.0 %collective-permute-start.1 = (f32[3,1,256]{2,1,0:T(1,128)S(1)}, f32[3,1,256]{2,1,0:T(1,128)S(1)}, u32[]{:S(2)}, u32[]{:S(2)}) collective-permute-start(f32[3,1,256]{2,1,0:T(1,128)S(1)} %get-tuple-element.77), channel_id=1, source_target_pairs={{16,0},{32,16},{48,32},{64,48},{80,64},{96,80},{112,96},{128,112},... | collective-permute-start | bytes 9224 | tf_op jit(solution)/shard_map/ppermute | solution.py:15
  38.6 61.5 %copy-start.25 = (pred[257]{0:T(512)(128)(4,1)}, pred[257]{0:T(512)(128)(4,1)S(1)}, u32[]{:S(2)}) copy-start(pred[257]{0:T(512)(128)(4,1)S(1)} %fusion.78) | copy-start | bytes 775
  39.4 9.4 %collective-permute-start.2 = (f32[3,66,1]{2,1,0:T(8,128)S(1)}, f32[3,66,1]{2,1,0:T(8,128)S(1)}, u32[]{:S(2)}, u32[]{:S(2)}) collective-permute-start(f32[3,66,1]{2,1,0:T(8,128)S(1)} %get-tuple-element.74), channel_id=1, source_target_pairs={{0,4},{4,8},{8,12},{1,5},{5,9},{9,13},{2,6},{6,10},{10,14},{3,7},{... | collective-permute-start | bytes 2384 | tf_op jit(solution)/shard_map/ppermute | solution.py:14
  42.2 6.6 %collective-permute-start.3 = (f32[3,66,1]{2,1,0:T(8,128)S(1)}, f32[3,66,1]{2,1,0:T(8,128)S(1)}, u32[]{:S(2)}, u32[]{:S(2)}) collective-permute-start(f32[3,66,1]{2,1,0:T(8,128)S(1)} %get-tuple-element.75), channel_id=1, source_target_pairs={{4,0},{8,4},{12,8},{5,1},{9,5},{13,9},{6,2},{10,6},{14,10},{7,3},{... | collective-permute-start | bytes 2384 | tf_op jit(solution)/shard_map/ppermute | solution.py:15
  43.5 5.6 %collective-permute-start.6 = (f32[2,5,1,128]{3,0,2,1:T(2,128)S(1)}, f32[2,5,1,128]{3,0,2,1:T(2,128)S(1)}, u32[]{:S(2)}, u32[]{:S(2)}) collective-permute-start(f32[2,5,1,128]{3,0,2,1:T(2,128)S(1)} %get-tuple-element.182), channel_id=1, source_target_pairs={{0,4},{4,8},{8,12},{1,5},{5,9},{9,13},{2,6},{6,10},{10,14},{3,7},{... | collective-permute-start | bytes 15368 | tf_op jit(solution)/shard_map/ppermute | solution.py:14
  47.5 4.4 %collective-permute-start.7 = (f32[2,5,1,128]{3,0,2,1:T(2,128)S(1)}, f32[2,5,1,128]{3,0,2,1:T(2,128)S(1)}, u32[]{:S(2)}, u32[]{:S(2)}) collective-permute-start(f32[2,5,1,128]{3,0,2,1:T(2,128)S(1)} %get-tuple-element.183), channel_id=1, source_target_pairs={{4,0},{8,4},{12,8},{5,1},{9,5},{13,9},{6,2},{10,6},{14,10},{7,3},{... | collective-permute-start | bytes 15368 | tf_op jit(solution)/shard_map/ppermute | solution.py:15
  66.7 9.2 %collective-permute-start.8 = (f32[13,1,256]{2,0,1:T(8,128)S(1)}, f32[13,1,256]{2,0,1:T(8,128)S(1)}, u32[]{:S(2)}, u32[]{:S(2)}) collective-permute-start(f32[13,1,256]{2,0,1:T(8,128)S(1)} %get-tuple-element.64), channel_id=1, source_target_pairs={{0,16},{16,32},{32,48},{48,64},{64,80},{80,96},{96,112},{112,128},... | collective-permute-start | bytes 39944 | tf_op jit(solution)/shard_map/ppermute | solution.py:14
  73.6 6.3 %collective-permute-start.9 = (f32[13,1,256]{2,0,1:T(8,128)S(1)}, f32[13,1,256]{2,0,1:T(8,128)S(1)}, u32[]{:S(2)}, u32[]{:S(2)}) collective-permute-start(f32[13,1,256]{2,0,1:T(8,128)S(1)} %get-tuple-element.65), channel_id=1, source_target_pairs={{16,0},{32,16},{48,32},{64,48},{80,64},{96,80},{112,96},{128,112},... | collective-permute-start | bytes 39944 | tf_op jit(solution)/shard_map/ppermute | solution.py:15
  80.1 4.8 %collective-permute-start.10 = (f32[13,18,1]{2,0,1:T(8,128)S(1)}, f32[13,18,1]{2,0,1:T(8,128)S(1)}, u32[]{:S(2)}, u32[]{:S(2)}) collective-permute-start(f32[13,18,1]{2,0,1:T(8,128)S(1)} %get-tuple-element.62), channel_id=1, source_target_pairs={{0,4},{4,8},{8,12},{1,5},{5,9},{9,13},{2,6},{6,10},{10,14},{3,7},{... | collective-permute-start | bytes 2816 | tf_op jit(solution)/shard_map/ppermute | solution.py:14
  82.8 5.9 %collective-permute-start.11 = (f32[13,18,1]{2,0,1:T(8,128)S(1)}, f32[13,18,1]{2,0,1:T(8,128)S(1)}, u32[]{:S(2)}, u32[]{:S(2)}) collective-permute-start(f32[13,18,1]{2,0,1:T(8,128)S(1)} %get-tuple-element.63), channel_id=1, source_target_pairs={{4,0},{8,4},{12,8},{5,1},{9,5},{13,9},{6,2},{10,6},{14,10},{7,3},{... | collective-permute-start | bytes 2816 | tf_op jit(solution)/shard_map/ppermute | solution.py:15
  89.2 5.9 %collective-permute-start.12 = (f32[4,1,18,258]{3,0,2,1:T(4,128)S(1)}, f32[4,1,18,258]{3,0,2,1:T(4,128)S(1)}, u32[]{:S(2)}, u32[]{:S(2)}) collective-permute-start(f32[4,1,18,258]{3,0,2,1:T(4,128)S(1)} %copy.245), channel_id=1, source_target_pairs={{0,1},{1,2},{2,3},{4,5},{5,6},{6,7},{8,9},{9,10},{10,11},{12,13},{... | collective-permute-start | bytes 222920 | tf_op jit(solution)/shard_map/ppermute | solution.py:14
  93.6 7.7 %collective-permute-start.13 = (f32[4,1,18,258]{3,0,2,1:T(4,128)S(1)}, f32[4,1,18,258]{3,0,2,1:T(4,128)S(1)}, u32[]{:S(2)}, u32[]{:S(2)}) collective-permute-start(f32[4,1,18,258]{3,0,2,1:T(4,128)S(1)} %copy.246), channel_id=1, source_target_pairs={{1,0},{2,1},{3,2},{5,4},{6,5},{7,6},{9,8},{10,9},{11,10},{13,12},{... | collective-permute-start | bytes 222920 | tf_op jit(solution)/shard_map/ppermute | solution.py:15
  100.0 15.1 %copy-start.6 = (f32[1,17,257]{2,0,1:T(1,128)}, f32[1,17,257]{2,0,1:T(1,128)S(1)}, u32[]{:S(2)}) copy-start(f32[1,17,257]{2,0,1:T(1,128)S(1)} %get-tuple-element.177) | copy-start | bytes 52432
  100.0 15.1 %copy-start.8 = (f32[1,17,257]{2,0,1:T(1,128)}, f32[1,17,257]{2,0,1:T(1,128)S(1)}, u32[]{:S(2)}) copy-start(f32[1,17,257]{2,0,1:T(1,128)S(1)} %get-tuple-element.178) | copy-start | bytes 52432
  100.1 19.7 %copy-start.4 = (f32[1,17,257]{2,0,1:T(1,128)}, f32[1,17,257]{2,0,1:T(1,128)S(1)}, u32[]{:S(2)}) copy-start(f32[1,17,257]{2,0,1:T(1,128)S(1)} %get-tuple-element.167) | copy-start | bytes 52432
  129.8 30.5 %copy-start.3 = (f32[64,256]{1,0:T(8,128)S(1)}, f32[64,256]{1,0:T(8,128)}, u32[]{:S(2)}) copy-start(f32[64,256]{1,0:T(8,128)} %param.13) | copy-start | bytes 196612
  154.4 8.9 %collective-permute-start.14 = (f32[2,1,3,128]{3,0,2,1:T(2,128)S(1)}, f32[2,1,3,128]{3,0,2,1:T(2,128)S(1)}, u32[]{:S(2)}, u32[]{:S(2)}) collective-permute-start(f32[2,1,3,128]{3,0,2,1:T(2,128)S(1)} %get-tuple-element.185), channel_id=1, source_target_pairs={{0,16},{16,32},{32,48},{48,64},{64,80},{80,96},{96,112},{112,128},... | collective-permute-start | bytes 9224 | tf_op jit(solution)/shard_map/ppermute | solution.py:14
  161.4 6.1 %collective-permute-start.15 = (f32[2,1,3,128]{3,0,2,1:T(2,128)S(1)}, f32[2,1,3,128]{3,0,2,1:T(2,128)S(1)}, u32[]{:S(2)}, u32[]{:S(2)}) collective-permute-start(f32[2,1,3,128]{3,0,2,1:T(2,128)S(1)} %get-tuple-element.184), channel_id=1, source_target_pairs={{16,0},{32,16},{48,32},{64,48},{80,64},{96,80},{112,96},{128,112},... | collective-permute-start | bytes 9224 | tf_op jit(solution)/shard_map/ppermute | solution.py:15
  167.5 6.3 %collective-permute-start.16 = (f32[2,5,1,128]{3,0,2,1:T(2,128)S(1)}, f32[2,5,1,128]{3,0,2,1:T(2,128)S(1)}, u32[]{:S(2)}, u32[]{:S(2)}) collective-permute-start(f32[2,5,1,128]{3,0,2,1:T(2,128)S(1)} %get-tuple-element.180), channel_id=1, source_target_pairs={{0,4},{4,8},{8,12},{1,5},{5,9},{9,13},{2,6},{6,10},{10,14},{3,7},{... | collective-permute-start | bytes 15368 | tf_op jit(solution)/shard_map/ppermute | solution.py:14
  170.8 4.4 %collective-permute-start.17 = (f32[2,5,1,128]{3,0,2,1:T(2,128)S(1)}, f32[2,5,1,128]{3,0,2,1:T(2,128)S(1)}, u32[]{:S(2)}, u32[]{:S(2)}) collective-permute-start(f32[2,5,1,128]{3,0,2,1:T(2,128)S(1)} %get-tuple-element.181), channel_id=1, source_target_pairs={{4,0},{8,4},{12,8},{5,1},{9,5},{13,9},{6,2},{10,6},{14,10},{7,3},{... | collective-permute-start | bytes 15368 | tf_op jit(solution)/shard_map/ppermute | solution.py:15
  (13 other events, 136.4 us)
where the time goes:
time: 203 us; the launch traced here: 201 us
  local copies, waits for them, and re-layouts  62.5 us (31%)
  starting transfers between devices  53.3 us (26%)
  other arithmetic  51.7 us (25%)
  waiting for transfers between devices  16.8 us (8%)
  blocking collectives  9.58 us (5%)
  matrix products  5.27 us (3%)
    ppermute x9, starting transfers between devices, with_halo(): before = lax.ppermute(last, axis, up)  39 us
    ppermute x9, waiting for transfers between devices, with_halo(): after = lax.ppermute(initial, axis, down)  16.2 us
    ppermute x9, starting transfers between devices, with_halo(): after = lax.ppermute(initial, axis, down)  14.3 us
    scatter-add x1, other arithmetic, per_device(): node_force = jnp.zeros((2, row_count * col_count + 1), jnp.float32).at[:,...  14 us
    another operation x8, local copies, waits for them, and re-layouts, triangle(): jnp.stack([plane[comp] for group in (lows, ups) for comp in range(3) for...  11.7 us
    unnamed x71, local copies, waits for them, and re-layouts  10.8 us
    scatter-add x1, other arithmetic, per_device(): placed = jnp.zeros((2, column_count + 1), jnp.float32).at[:, target].add(...  10.6 us
    psum x1, blocking collectives, per_device(): depth_total = lax.psum(bucket, 'layer')  9.58 us
  transfers between devices with their start and end apart: 18, of which 6 were waited for; matrix products, arithmetic and copies ran while one was open for 10% of the time, Pallas kernels for 0%

commit v1 on v0

--- a/solution.py
+++ b/solution.py
@@ -192,7 +192,7 @@
     stokes_residual = jnp.stack(owned, axis=1) - body_force
     depth_sum = jnp.sum(stokes_residual[:2], axis=1).reshape(2, column_count)
     bucket = jnp.where(col_live[None], depth_sum[:, jnp.maximum(columns, 0)], 0.0)
-    depth_total = lax.psum(bucket, "layer")
+    depth_total = jnp.sum(lax.all_gather(bucket, "layer"), axis=0)
     grid_back = depth_total.reshape(2, 3, 3, slot_count)
     extended_back = with_halo(grid_back, (("mx", 1), ("my", 2)), 1)
     at_owner = extended_back[:, 0::2, 0::2].reshape(2, 9, slot_count)

time: 203 us -> 199 us (0.980)
  local copies, waits for them, and re-layouts: 62.5 us -> 59.4 us
    all_gather x0 -> x1, blocking collectives: none -> 10.2 us  [per_device(): depth_total = jnp.sum(lax.all_gather(bucket, 'layer'), axis=0)]
    psum x1 -> x0, blocking collectives: 9.58 us -> none  [per_device(): depth_total = lax.psum(bucket, 'layer')]
    unnamed x71 -> x67, local copies, waits for them, and re-layouts: 10.8 us -> 8.49 us
    slice x15 -> x10, local copies, waits for them, and re-layouts: 5.54 us -> 4.38 us  [triangle(): plane[comp]]
where the time goes in v1:
time: 199 us; the launch traced here: 197 us
  local copies, waits for them, and re-layouts  59.4 us (30%)
  starting transfers between devices  54.2 us (27%)
  other arithmetic  49.7 us (25%)
  waiting for transfers between devices  15.8 us (8%)
  blocking collectives  10.2 us (5%)
  matrix products  6.07 us (3%)
    ppermute x9, starting transfers between devices, with_halo(): before = lax.ppermute(last, axis, up)  39.9 us
    ppermute x9, waiting for transfers between devices, with_halo(): after = lax.ppermute(initial, axis, down)  15.2 us
    ppermute x9, starting transfers between devices, with_halo(): after = lax.ppermute(initial, axis, down)  14.3 us
    scatter-add x1, other arithmetic, per_device(): node_force = jnp.zeros((2, row_count * col_count + 1), jnp.float32).at[:,...  14 us
    another operation x8, local copies, waits for them, and re-layouts, triangle(): jnp.stack([plane[comp] for group in (lows, ups) for comp in range(3) for...  12.4 us
    scatter-add x1, other arithmetic, per_device(): placed = jnp.zeros((2, column_count + 1), jnp.float32).at[:, target].add(...  10.6 us
    all_gather x1, blocking collectives, per_device(): depth_total = jnp.sum(lax.all_gather(bucket, 'layer'), axis=0)  10.2 us
    scatter-add x1, other arithmetic, per_device(): jnp.zeros((column_count + 1,), jnp.float32).at[target].add(1.0)  8.69 us
  transfers between devices with their start and end apart: 18, of which 6 were waited for; matrix products, arithmetic and copies ran while one was open for 10% of the time, Pallas kernels for 0%

profile of v1, /device:TPU:97, one launch (start us, length us, event | category | flops | bytes accessed | tf_op | source)
XLA Modules:
  0.0 197.3 jit_solution(15354366289654764724)
XLA Ops:
  2.2 5.5 %copy.172 = f32[2,64,256]{0,2,1:T(8,128)} copy(f32[2,64,256]{2,1,0:T(8,128)} %param.11) | data formatting | bytes 262144 | tf_op args[0]
  7.8 5.9 %gather_fusion = f32[1152,2]{1,0:T(8,128)S(1)} fusion(f32[2,16384]{0,1:T(8,128)} %bitcast.291, s32[2048]{0:T(1024)S(1)} %pad_clamp_fusion.1), kind=kCustom, calls=%fused_computation | custom fusion | bytes 23040 | tf_op jit(solution)/shard_map/gather | solution.py:126
  13.9 5.3 %collective-permute-start.4 = (f32[2,1,3,128]{3,0,2,1:T(2,128)S(1)}, f32[2,1,3,128]{3,0,2,1:T(2,128)S(1)}, u32[]{:S(2)}, u32[]{:S(2)}) collective-permute-start(f32[2,1,3,128]{3,0,2,1:T(2,128)S(1)} %get-tuple-element.196), channel_id=1, source_target_pairs={{0,16},{16,32},{32,48},{48,64},{64,80},{80,96},{96,112},{112,128},... | collective-permute-start | bytes 9224 | tf_op jit(solution)/shard_map/ppermute | solution.py:14
  19.2 1.9 collective-permute-start.5
  21.2 4.9 %collective-permute-start = (f32[3,1,256]{2,1,0:T(1,128)S(1)}, f32[3,1,256]{2,1,0:T(1,128)S(1)}, u32[]{:S(2)}, u32[]{:S(2)}) collective-permute-start(f32[3,1,256]{2,1,0:T(1,128)S(1)} %get-tuple-element.76), channel_id=1, source_target_pairs={{0,16},{16,32},{32,48},{48,64},{64,80},{80,96},{96,112},{112,128},... | collective-permute-start | bytes 9224 | tf_op jit(solution)/shard_map/ppermute | solution.py:14
  26.0 1.9 collective-permute-start.1
  28.7 8.7 %scatter_custom_fusion = f32[4097]{0:T(1024)S(1)} fusion(s32[1152]{0:T(1024)S(1)} %fusion.75, f32[1152]{0:T(1024)S(1)} %broadcast.313, f32[]{:T(128)} %constant.32.clone.1), kind=kCustom, calls=%fused_computation.251 | custom fusion | flops 1152 | bytes 16392 | tf_op jit(solution)/shard_map/scatter-add | solution.py:143
  38.8 2.8 %collective-permute-start.2 = (f32[3,66,1]{2,1,0:T(8,128)S(1)}, f32[3,66,1]{2,1,0:T(8,128)S(1)}, u32[]{:S(2)}, u32[]{:S(2)}) collective-permute-start(f32[3,66,1]{2,1,0:T(8,128)S(1)} %get-tuple-element.74), channel_id=1, source_target_pairs={{0,4},{4,8},{8,12},{1,5},{5,9},{9,13},{2,6},{6,10},{10,14},{3,7},{... | collective-permute-start | bytes 2384 | tf_op jit(solution)/shard_map/ppermute | solution.py:14
  42.9 4.0 %collective-permute-start.6 = (f32[2,5,1,128]{3,0,2,1:T(2,128)S(1)}, f32[2,5,1,128]{3,0,2,1:T(2,128)S(1)}, u32[]{:S(2)}, u32[]{:S(2)}) collective-permute-start(f32[2,5,1,128]{3,0,2,1:T(2,128)S(1)} %get-tuple-element.182), channel_id=1, source_target_pairs={{0,4},{4,8},{8,12},{1,5},{5,9},{9,13},{2,6},{6,10},{10,14},{3,7},{... | collective-permute-start | bytes 15368 | tf_op jit(solution)/shard_map/ppermute | solution.py:14
  48.5 2.8 %collective-permute-done.7 = f32[2,5,1,128]{3,0,2,1:T(2,128)S(1)} collective-permute-done((f32[2,5,1,128]{3,0,2,1:T(2,128)S(1)}, f32[2,5,1,128]{3,0,2,1:T(2,128)S(1)}, u32[]{:S(2)}, u32[]{:S(2)}) %collective-permute-start.7) | collective-permute-done | bytes 5152 | tf_op jit(solution)/shard_map/ppermute | solution.py:15
  51.6 10.6 %scatter_custom_fusion.1 = f32[2,4097]{0,1:T(8,128)S(1)} fusion(s32[1152]{0:T(1024)S(1)} %fusion.75, f32[1152,2]{1,0:T(8,128)S(1)} %copy.174, f32[]{:T(128)} %constant.32.clone.1), kind=kCustom, calls=%fused_computation.23 | custom fusion | flops 2304 | bytes 32780 | tf_op jit(solution)/shard_map/scatter-add | solution.py:141
  62.2 1.5 slice.1284
  63.6 2.2 %copy.175 = f32[2,16,256]{2,1,0:T(8,128)S(1)} copy(f32[2,16,256]{0,2,1:T(8,128)} %bitcast.292) | data formatting | bytes 65536 | tf_op jit(solution)/shard_map/jit(_where)/broadcast_in_dim | solution.py:144
  66.1 7.0 %collective-permute-start.8 = (f32[13,1,256]{2,0,1:T(8,128)S(1)}, f32[13,1,256]{2,0,1:T(8,128)S(1)}, u32[]{:S(2)}, u32[]{:S(2)}) collective-permute-start(f32[13,1,256]{2,0,1:T(8,128)S(1)} %get-tuple-element.64), channel_id=1, source_target_pairs={{0,16},{16,32},{32,48},{48,64},{64,80},{80,96},{96,112},{112,128},... | collective-permute-start | bytes 39944 | tf_op jit(solution)/shard_map/ppermute | solution.py:14
  73.0 1.9 collective-permute-start.9
  75.2 4.1 %collective-permute-done.9 = f32[13,1,256]{2,0,1:T(8,128)S(1)} collective-permute-done((f32[13,1,256]{2,0,1:T(8,128)S(1)}, f32[13,1,256]{2,0,1:T(8,128)S(1)}, u32[]{:S(2)}, u32[]{:S(2)}) %collective-permute-start.9) | collective-permute-done | bytes 13344 | tf_op jit(solution)/shard_map/ppermute | solution.py:15
  79.4 2.7 %collective-permute-start.10 = (f32[13,18,1]{2,0,1:T(8,128)S(1)}, f32[13,18,1]{2,0,1:T(8,128)S(1)}, u32[]{:S(2)}, u32[]{:S(2)}) collective-permute-start(f32[13,18,1]{2,0,1:T(8,128)S(1)} %get-tuple-element.62), channel_id=1, source_target_pairs={{0,4},{4,8},{8,12},{1,5},{5,9},{9,13},{2,6},{6,10},{10,14},{3,7},{... | collective-permute-start | bytes 2816 | tf_op jit(solution)/shard_map/ppermute | solution.py:14
  84.3 3.8 %collective-permute-done.11 = f32[13,18,1]{2,0,1:T(8,128)S(1)} collective-permute-done((f32[13,18,1]{2,0,1:T(8,128)S(1)}, f32[13,18,1]{2,0,1:T(8,128)S(1)}, u32[]{:S(2)}, u32[]{:S(2)}) %collective-permute-start.11) | collective-permute-done | bytes 968 | tf_op jit(solution)/shard_map/ppermute | solution.py:15
  88.6 3.1 %collective-permute-start.12 = (f32[4,1,18,258]{3,0,2,1:T(4,128)S(1)}, f32[4,1,18,258]{3,0,2,1:T(4,128)S(1)}, u32[]{:S(2)}, u32[]{:S(2)}) collective-permute-start(f32[4,1,18,258]{3,0,2,1:T(4,128)S(1)} %copy.245), channel_id=1, source_target_pairs={{0,1},{1,2},{2,3},{4,5},{5,6},{6,7},{8,9},{9,10},{10,11},{12,13},{... | collective-permute-start | bytes 222920 | tf_op jit(solution)/shard_map/ppermute | solution.py:14
  99.8 1.9 and_select_fusion.1
  103.6 2.3 %stack.48 = f32[18,17,257]{2,0,1:T(8,128)S(1)} concatenate(f32[1,17,257]{2,0,1:T(1,128)} %get-tuple-element.106, f32[1,17,257]{2,0,1:T(1,128)} %get-tuple-element.105, f32[1,17,257]{2,0,1:T(1,128)} %get-tuple-element.152, f32[1,17,257]{2,0,1:T(1,128)} %get-tuple-element.103, f32[1,17,257]{2,0,1:T(1,128)} %get-tuple-element.102, f32[1,17,257]{2,0,1:T(1,128)} %get-tuple-element.151, ...), dimensions={0} | concatenate | bytes 629136 | tf_op jit(solution)/shard_map/stack | solution.py:46
  123.0 3.0 %stack.56 = f32[18,17,257]{2,0,1:T(8,128)S(1)} concatenate(f32[1,17,257]{2,0,1:T(1,128)} %copy-done.8, f32[1,17,257]{2,0,1:T(1,128)S(1)} %copy-done.7, f32[1,17,257]{2,0,1:T(1,128)S(1)} %get-tuple-element.167, f32[1,17,257]{2,0,1:T(1,128)S(1)} %copy-done.5, f32[1,17,257]{2,0,1:T(1,128)S(1)} %get-tuple-element.139, f32[1,17,257]{2,0,1:T(1,128)S(1)} %get-tuple-element.166, ...), dimensions={0} | concatenate | bytes 629136 | tf_op jit(solution)/shard_map/stack | solution.py:46
  129.0 2.3 %stack.57 = f32[18,17,257]{2,0,1:T(8,128)S(1)} concatenate(f32[1,17,257]{2,0,1:T(1,128)S(1)} %get-tuple-element.204, f32[1,17,257]{2,0,1:T(1,128)S(1)} %get-tuple-element.137, f32[1,17,257]{2,0,1:T(1,128)S(1)} %get-tuple-element.118, f32[1,17,257]{2,0,1:T(1,128)S(1)} %get-tuple-element.205, f32[1,17,257]{2,0,1:T(1,128)S(1)} %get-tuple-element.117, ...), dimensions={0} | concatenate | bytes 629136 | tf_op jit(solution)/shard_map/stack | solution.py:46
  137.7 2.4 %gather_fusion.1 = f32[1152,2]{1,0:T(8,128)S(1)} fusion(f32[2,4096]{0,1:T(8,128)S(1)} %bitcast.299, s32[2048]{0:T(1024)S(1)} %copy-done.23), kind=kCustom, calls=%fused_computation.1 | custom fusion | bytes 23040 | tf_op jit(solution)/shard_map/gather | solution.py:194
  140.4 10.2 %all_gather.4 = f32[4,2,9,128]{3,1,2,0:T(2,128)S(1)} all-gather(f32[1,2,9,128]{3,1,2,0:T(2,128)S(1)} %bitcast_select_fusion), channel_id=1, replica_groups=mesh['mx'=32,'my'=4,'layer'=4] {'layer'}, dimensions={0}, use_global_device_ids=true | all-gather | bytes 46080 | tf_op jit(solution)/shard_map/all_gather | solution.py:195
  150.7 6.8 %collective-permute-start.14 = (f32[2,1,3,128]{3,0,2,1:T(2,128)S(1)}, f32[2,1,3,128]{3,0,2,1:T(2,128)S(1)}, u32[]{:S(2)}, u32[]{:S(2)}) collective-permute-start(f32[2,1,3,128]{3,0,2,1:T(2,128)S(1)} %get-tuple-element.184), channel_id=1, source_target_pairs={{0,16},{16,32},{32,48},{48,64},{64,80},{80,96},{96,112},{112,128},... | collective-permute-start | bytes 9224 | tf_op jit(solution)/shard_map/ppermute | solution.py:14
  157.5 1.9 collective-permute-start.15
  160.5 3.2 %collective-permute-done.15 = f32[2,1,3,128]{3,0,2,1:T(2,128)S(1)} collective-permute-done((f32[2,1,3,128]{3,0,2,1:T(2,128)S(1)}, f32[2,1,3,128]{3,0,2,1:T(2,128)S(1)}, u32[]{:S(2)}, u32[]{:S(2)}) %collective-permute-start.15) | collective-permute-done | bytes 3104 | tf_op jit(solution)/shard_map/ppermute | solution.py:15
  163.7 3.3 %collective-permute-start.16 = (f32[2,5,1,128]{3,0,2,1:T(2,128)S(1)}, f32[2,5,1,128]{3,0,2,1:T(2,128)S(1)}, u32[]{:S(2)}, u32[]{:S(2)}) collective-permute-start(f32[2,5,1,128]{3,0,2,1:T(2,128)S(1)} %get-tuple-element.180), channel_id=1, source_target_pairs={{0,4},{4,8},{8,12},{1,5},{5,9},{9,13},{2,6},{6,10},{10,14},{3,7},{... | collective-permute-start | bytes 15368 | tf_op jit(solution)/shard_map/ppermute | solution.py:14
  171.6 14.0 %scatter_custom_fusion.2 = f32[2,16385]{0,1:T(8,128)} fusion(s32[1152]{0:T(1024)} %fusion.74, f32[1152,2]{1,0:T(8,128)S(1)} %copy.231, f32[]{:T(128)} %constant.32.clone.1), kind=kCustom, calls=%fused_computation.5 | custom fusion | flops 2304 | bytes 131592 | tf_op jit(solution)/shard_map/scatter-add | solution.py:203
  185.6 5.7 %slice.1541 = f32[2,16384]{0,1:T(8,128)} slice(f32[2,16385]{0,1:T(8,128)} %scatter_custom_fusion.2), slice={[0:2], [0:16384]} | slice | bytes 262144 | tf_op jit(solution)/shard_map/slice | solution.py:205
  191.4 5.2 %copy.232 = f32[2,64,256]{2,1,0:T(8,128)S(1)} copy(f32[2,64,256]{0,2,1:T(8,128)} %bitcast.278) | data formatting | bytes 262144 | tf_op jit(solution)/shard_map/reshape | solution.py:205
  (205 shorter events, 52.5 us)
Async XLA Ops:
  0.6 105.2 %copy-start = (f32[18,18]{1,0:T(8,128)S(1)}, f32[18,18]{1,0:T(8,128)}, u32[]{:S(2)}) copy-start(f32[18,18]{1,0:T(8,128)} %param.19) | copy-start | bytes 3892
  0.6 27.4 %copy-start.22 = (s32[1,9,128]{2,0,1:T(1,128)S(1)}, s32[1,9,128]{2,0,1:T(1,128)}, u32[]{:S(2)}) copy-start(s32[1,9,128]{2,0,1:T(1,128)} %param.21) | copy-start | bytes 13828
  0.7 20.5 %copy-start.1 = (f32[2,64,256]{2,1,0:T(8,128)S(1)}, f32[2,64,256]{2,1,0:T(8,128)}, u32[]{:S(2)}) copy-start(f32[2,64,256]{2,1,0:T(8,128)} %param.11) | copy-start | bytes 393220
  0.7 20.5 %copy-start.2 = (f32[64,256]{1,0:T(8,128)S(1)}, f32[64,256]{1,0:T(8,128)}, u32[]{:S(2)}) copy-start(f32[64,256]{1,0:T(8,128)} %param.12) | copy-start | bytes 196612
  0.7 27.3 %copy-start.21 = (s32[1,9,128]{2,0,1:T(1,128)S(1)}, s32[1,9,128]{2,0,1:T(1,128)}, u32[]{:S(2)}) copy-start(s32[1,9,128]{2,0,1:T(1,128)} %param.20) | copy-start | bytes 13828
  0.7 37.4 %copy-start.24 = (s32[16,256]{1,0:T(8,128)S(1)}, s32[16,256]{1,0:T(8,128)}, u32[]{:S(2)}) copy-start(s32[16,256]{1,0:T(8,128)} %param.18) | copy-start | bytes 49156
  7.7 58.1 %copy-start.10 = (f32[3,3,16,256]{3,2,1,0:T(8,128)S(1)}, f32[3,3,16,256]{3,2,1,0:T(8,128)}, u32[]{:S(2)}) copy-start(f32[3,3,16,256]{3,2,1,0:T(8,128)} %param.15) | copy-start | bytes 442372
  7.8 58.1 %slice-start = ((f32[3,3,16,256]{3,2,1,0:T(8,128)}), f32[1,3,16,256]{3,2,1,0:T(8,128)S(1)}, s32[]{:S(2)}) async-start(f32[3,3,16,256]{3,2,1,0:T(8,128)} %param.15), calls=%async_computation | async-start | bytes 98304 | tf_op jit(solution)/shard_map/slice | solution.py:149
  7.8 58.1 %copy-start.20 = (f32[3,16,256]{2,1,0:T(8,128)S(1)}, f32[3,16,256]{2,1,0:T(8,128)}, u32[]{:S(2)}) copy-start(f32[3,16,256]{2,1,0:T(8,128)} %param.16) | copy-start | bytes 147460
  13.9 29.0 %collective-permute-start.4 = (f32[2,1,3,128]{3,0,2,1:T(2,128)S(1)}, f32[2,1,3,128]{3,0,2,1:T(2,128)S(1)}, u32[]{:S(2)}, u32[]{:S(2)}) collective-permute-start(f32[2,1,3,128]{3,0,2,1:T(2,128)S(1)} %get-tuple-element.196), channel_id=1, source_target_pairs={{0,16},{16,32},{32,48},{48,64},{64,80},{80,96},{96,112},{112,128},... | collective-permute-start | bytes 9224 | tf_op jit(solution)/shard_map/ppermute | solution.py:14
  19.2 23.7 %collective-permute-start.5 = (f32[2,1,3,128]{3,0,2,1:T(2,128)S(1)}, f32[2,1,3,128]{3,0,2,1:T(2,128)S(1)}, u32[]{:S(2)}, u32[]{:S(2)}) collective-permute-start(f32[2,1,3,128]{3,0,2,1:T(2,128)S(1)} %get-tuple-element.197), channel_id=1, source_target_pairs={{16,0},{32,16},{48,32},{64,48},{80,64},{96,80},{112,96},{128,112},... | collective-permute-start | bytes 9224 | tf_op jit(solution)/shard_map/ppermute | solution.py:15
  21.2 17.5 %collective-permute-start = (f32[3,1,256]{2,1,0:T(1,128)S(1)}, f32[3,1,256]{2,1,0:T(1,128)S(1)}, u32[]{:S(2)}, u32[]{:S(2)}) collective-permute-start(f32[3,1,256]{2,1,0:T(1,128)S(1)} %get-tuple-element.76), channel_id=1, source_target_pairs={{0,16},{16,32},{32,48},{48,64},{64,80},{80,96},{96,112},{112,128},... | collective-permute-start | bytes 9224 | tf_op jit(solution)/shard_map/ppermute | solution.py:14
  26.0 12.6 %collective-permute-start.1 = (f32[3,1,256]{2,1,0:T(1,128)S(1)}, f32[3,1,256]{2,1,0:T(1,128)S(1)}, u32[]{:S(2)}, u32[]{:S(2)}) collective-permute-start(f32[3,1,256]{2,1,0:T(1,128)S(1)} %get-tuple-element.77), channel_id=1, source_target_pairs={{16,0},{32,16},{48,32},{64,48},{80,64},{96,80},{112,96},{128,112},... | collective-permute-start | bytes 9224 | tf_op jit(solution)/shard_map/ppermute | solution.py:15
  38.0 60.1 %copy-start.25 = (pred[257]{0:T(512)(128)(4,1)}, pred[257]{0:T(512)(128)(4,1)S(1)}, u32[]{:S(2)}) copy-start(pred[257]{0:T(512)(128)(4,1)S(1)} %fusion.78) | copy-start | bytes 775
  38.8 9.4 %collective-permute-start.2 = (f32[3,66,1]{2,1,0:T(8,128)S(1)}, f32[3,66,1]{2,1,0:T(8,128)S(1)}, u32[]{:S(2)}, u32[]{:S(2)}) collective-permute-start(f32[3,66,1]{2,1,0:T(8,128)S(1)} %get-tuple-element.74), channel_id=1, source_target_pairs={{0,4},{4,8},{8,12},{1,5},{5,9},{9,13},{2,6},{6,10},{10,14},{3,7},{... | collective-permute-start | bytes 2384 | tf_op jit(solution)/shard_map/ppermute | solution.py:14
  41.6 6.6 %collective-permute-start.3 = (f32[3,66,1]{2,1,0:T(8,128)S(1)}, f32[3,66,1]{2,1,0:T(8,128)S(1)}, u32[]{:S(2)}, u32[]{:S(2)}) collective-permute-start(f32[3,66,1]{2,1,0:T(8,128)S(1)} %get-tuple-element.75), channel_id=1, source_target_pairs={{4,0},{8,4},{12,8},{5,1},{9,5},{13,9},{6,2},{10,6},{14,10},{7,3},{... | collective-permute-start | bytes 2384 | tf_op jit(solution)/shard_map/ppermute | solution.py:15
  42.9 5.6 %collective-permute-start.6 = (f32[2,5,1,128]{3,0,2,1:T(2,128)S(1)}, f32[2,5,1,128]{3,0,2,1:T(2,128)S(1)}, u32[]{:S(2)}, u32[]{:S(2)}) collective-permute-start(f32[2,5,1,128]{3,0,2,1:T(2,128)S(1)} %get-tuple-element.182), channel_id=1, source_target_pairs={{0,4},{4,8},{8,12},{1,5},{5,9},{9,13},{2,6},{6,10},{10,14},{3,7},{... | collective-permute-start | bytes 15368 | tf_op jit(solution)/shard_map/ppermute | solution.py:14
  46.9 4.4 %collective-permute-start.7 = (f32[2,5,1,128]{3,0,2,1:T(2,128)S(1)}, f32[2,5,1,128]{3,0,2,1:T(2,128)S(1)}, u32[]{:S(2)}, u32[]{:S(2)}) collective-permute-start(f32[2,5,1,128]{3,0,2,1:T(2,128)S(1)} %get-tuple-element.183), channel_id=1, source_target_pairs={{4,0},{8,4},{12,8},{5,1},{9,5},{13,9},{6,2},{10,6},{14,10},{7,3},{... | collective-permute-start | bytes 15368 | tf_op jit(solution)/shard_map/ppermute | solution.py:15
  66.1 9.2 %collective-permute-start.8 = (f32[13,1,256]{2,0,1:T(8,128)S(1)}, f32[13,1,256]{2,0,1:T(8,128)S(1)}, u32[]{:S(2)}, u32[]{:S(2)}) collective-permute-start(f32[13,1,256]{2,0,1:T(8,128)S(1)} %get-tuple-element.64), channel_id=1, source_target_pairs={{0,16},{16,32},{32,48},{48,64},{64,80},{80,96},{96,112},{112,128},... | collective-permute-start | bytes 39944 | tf_op jit(solution)/shard_map/ppermute | solution.py:14
  73.0 6.3 %collective-permute-start.9 = (f32[13,1,256]{2,0,1:T(8,128)S(1)}, f32[13,1,256]{2,0,1:T(8,128)S(1)}, u32[]{:S(2)}, u32[]{:S(2)}) collective-permute-start(f32[13,1,256]{2,0,1:T(8,128)S(1)} %get-tuple-element.65), channel_id=1, source_target_pairs={{16,0},{32,16},{48,32},{64,48},{80,64},{96,80},{112,96},{128,112},... | collective-permute-start | bytes 39944 | tf_op jit(solution)/shard_map/ppermute | solution.py:15
  79.4 4.8 %collective-permute-start.10 = (f32[13,18,1]{2,0,1:T(8,128)S(1)}, f32[13,18,1]{2,0,1:T(8,128)S(1)}, u32[]{:S(2)}, u32[]{:S(2)}) collective-permute-start(f32[13,18,1]{2,0,1:T(8,128)S(1)} %get-tuple-element.62), channel_id=1, source_target_pairs={{0,4},{4,8},{8,12},{1,5},{5,9},{9,13},{2,6},{6,10},{10,14},{3,7},{... | collective-permute-start | bytes 2816 | tf_op jit(solution)/shard_map/ppermute | solution.py:14
  82.2 5.9 %collective-permute-start.11 = (f32[13,18,1]{2,0,1:T(8,128)S(1)}, f32[13,18,1]{2,0,1:T(8,128)S(1)}, u32[]{:S(2)}, u32[]{:S(2)}) collective-permute-start(f32[13,18,1]{2,0,1:T(8,128)S(1)} %get-tuple-element.63), channel_id=1, source_target_pairs={{4,0},{8,4},{12,8},{5,1},{9,5},{13,9},{6,2},{10,6},{14,10},{7,3},{... | collective-permute-start | bytes 2816 | tf_op jit(solution)/shard_map/ppermute | solution.py:15
  88.6 5.9 %collective-permute-start.12 = (f32[4,1,18,258]{3,0,2,1:T(4,128)S(1)}, f32[4,1,18,258]{3,0,2,1:T(4,128)S(1)}, u32[]{:S(2)}, u32[]{:S(2)}) collective-permute-start(f32[4,1,18,258]{3,0,2,1:T(4,128)S(1)} %copy.245), channel_id=1, source_target_pairs={{0,1},{1,2},{2,3},{4,5},{5,6},{6,7},{8,9},{9,10},{10,11},{12,13},{... | collective-permute-start | bytes 222920 | tf_op jit(solution)/shard_map/ppermute | solution.py:14
  92.3 23.7 %copy-start.4 = (f32[1,17,257]{2,0,1:T(1,128)}, f32[1,17,257]{2,0,1:T(1,128)S(1)}, u32[]{:S(2)}) copy-start(f32[1,17,257]{2,0,1:T(1,128)S(1)} %get-tuple-element.140) | copy-start | bytes 52432
  92.3 23.7 %copy-start.6 = (f32[1,17,257]{2,0,1:T(1,128)}, f32[1,17,257]{2,0,1:T(1,128)S(1)}, u32[]{:S(2)}) copy-start(f32[1,17,257]{2,0,1:T(1,128)S(1)} %get-tuple-element.141) | copy-start | bytes 52432
  92.4 23.7 %copy-start.8 = (f32[1,17,257]{2,0,1:T(1,128)}, f32[1,17,257]{2,0,1:T(1,128)S(1)}, u32[]{:S(2)}) copy-start(f32[1,17,257]{2,0,1:T(1,128)S(1)} %get-tuple-element.142) | copy-start | bytes 52432
  93.1 6.5 %collective-permute-start.13 = (f32[4,1,18,258]{3,0,2,1:T(4,128)S(1)}, f32[4,1,18,258]{3,0,2,1:T(4,128)S(1)}, u32[]{:S(2)}, u32[]{:S(2)}) collective-permute-start(f32[4,1,18,258]{3,0,2,1:T(4,128)S(1)} %copy.246), channel_id=1, source_target_pairs={{1,0},{2,1},{3,2},{5,4},{6,5},{7,6},{9,8},{10,9},{11,10},{13,12},{... | collective-permute-start | bytes 222920 | tf_op jit(solution)/shard_map/ppermute | solution.py:15
  126.0 33.5 %copy-start.3 = (f32[64,256]{1,0:T(8,128)S(1)}, f32[64,256]{1,0:T(8,128)}, u32[]{:S(2)}) copy-start(f32[64,256]{1,0:T(8,128)} %param.13) | copy-start | bytes 196612
  150.7 9.8 %collective-permute-start.14 = (f32[2,1,3,128]{3,0,2,1:T(2,128)S(1)}, f32[2,1,3,128]{3,0,2,1:T(2,128)S(1)}, u32[]{:S(2)}, u32[]{:S(2)}) collective-permute-start(f32[2,1,3,128]{3,0,2,1:T(2,128)S(1)} %get-tuple-element.184), channel_id=1, source_target_pairs={{0,16},{16,32},{32,48},{48,64},{64,80},{80,96},{96,112},{112,128},... | collective-permute-start | bytes 9224 | tf_op jit(solution)/shard_map/ppermute | solution.py:14
  157.5 6.1 %collective-permute-start.15 = (f32[2,1,3,128]{3,0,2,1:T(2,128)S(1)}, f32[2,1,3,128]{3,0,2,1:T(2,128)S(1)}, u32[]{:S(2)}, u32[]{:S(2)}) collective-permute-start(f32[2,1,3,128]{3,0,2,1:T(2,128)S(1)} %get-tuple-element.185), channel_id=1, source_target_pairs={{16,0},{32,16},{48,32},{64,48},{80,64},{96,80},{112,96},{128,112},... | collective-permute-start | bytes 9224 | tf_op jit(solution)/shard_map/ppermute | solution.py:15
  163.7 6.3 %collective-permute-start.16 = (f32[2,5,1,128]{3,0,2,1:T(2,128)S(1)}, f32[2,5,1,128]{3,0,2,1:T(2,128)S(1)}, u32[]{:S(2)}, u32[]{:S(2)}) collective-permute-start(f32[2,5,1,128]{3,0,2,1:T(2,128)S(1)} %get-tuple-element.180), channel_id=1, source_target_pairs={{0,4},{4,8},{8,12},{1,5},{5,9},{9,13},{2,6},{6,10},{10,14},{3,7},{... | collective-permute-start | bytes 15368 | tf_op jit(solution)/shard_map/ppermute | solution.py:14
  167.0 4.4 %collective-permute-start.17 = (f32[2,5,1,128]{3,0,2,1:T(2,128)S(1)}, f32[2,5,1,128]{3,0,2,1:T(2,128)S(1)}, u32[]{:S(2)}, u32[]{:S(2)}) collective-permute-start(f32[2,5,1,128]{3,0,2,1:T(2,128)S(1)} %get-tuple-element.181), channel_id=1, source_target_pairs={{4,0},{8,4},{12,8},{5,1},{9,5},{13,9},{6,2},{10,6},{14,10},{7,3},{... | collective-permute-start | bytes 15368 | tf_op jit(solution)/shard_map/ppermute | solution.py:15
  (14 other events, 142.2 us)
